TPU v7x, 512 devices: a whole 4x4x16 slice. The times are simulated.
512 devices in a mesh: dp: 8 (over z_lo), seq: 4 (over z_hi, core), expert: 16 (over x, y).
Axes of the slice: x: 4, y: 4, z: 16 (z_hi: 2, z_lo: 8; z = z_hi * 8 + z_lo), core: 2. Of those that a mesh axis runs over, the one named last changes fastest.
Arguments:
- keys: bfloat16 [16, 4096, 512], P('expert', ('dp', 'seq')), may hold values from -4 to 4
- values: bfloat16 [16, 4096, 512], P('expert', ('dp', 'seq')), may hold values from -5 to 5
- queries: bfloat16 [16, 32, 4096], P('expert', ('dp', 'seq')), may hold values from -80 to 80
- residual: bfloat16 [16, 32, 2048], P('expert', ('dp', 'seq')), may hold values from -9 to 9
- out_proj: bfloat16 [4096, 2048], P(('dp', 'seq')), may hold values from -0.09375 to 0.09375
- norm_gain: bfloat16 [2048], replicated, may hold values from 0.25 to 1.75
- router: bfloat16 [2048, 128], replicated, may hold values from -8 to 8
- w_gate: bfloat16 [128, 2048, 768], P(('dp', 'expert'), None, 'seq'), may hold values from -0.125 to 0.125
- w_up: bfloat16 [128, 2048, 768], P(('dp', 'expert'), None, 'seq'), may hold values from -0.125 to 0.125
- w_down: bfloat16 [128, 768, 2048], P(('dp', 'expert'), 'seq'), may hold values from -0.21875 to 0.21875
- head_vec: bfloat16 [2048], replicated, may hold values from -0.09 to 0.09
- routes: int32 [16, 32, 8], P('expert', 'dp'), may hold values from 0 to 127, all different within a row; in each aligned block of 4 rows (0 to 3, 4 to 7, ..., all dimensions but the last counted through in order) at most 2 rows name the same one
- step_pos: int32 [16, 32], P('expert'), may hold values from 0 to 4095, as said below
- labels: int32 [16, 32], P('expert', ('dp', 'seq')), may hold values 0 or 1
- trace_len: int32 [16, 8], P('expert'), may hold values from 1 to 1024, 4096 in all within a row
Outputs:
- loss: float32 [], replicated
- grad_down: bfloat16 [128, 768, 2048], P(('dp', 'expert'), 'seq')
- grad_router: bfloat16 [2048, 128], P(('dp', 'seq', 'expert'))
Inputs may be any that keep to these rules, and one draw needn't show every extreme that they name: `step_pos`: increasing along each pack; distinct. `routes`: in each aligned block of 4 step ends (those of one index of dp in one pack) no expert is named by more than 2 of them.
All inputs are finite; a program needn't handle non-finite values. No bound on the sum of `labels` on one device may be relied on, other than what follows from the above.
Results may differ from a plain program's by a relative error of at most 0.018.
Values may be sent and summed in bfloat16 or wider, within the bound.
No kernel may reach another device: no remote copies, remote signals or barrier semaphores. Data moves between devices by JAX's collectives and lax.ppermute only.
A program may use at most 64 MiB of HBM per device.

v0:
```python
import jax
import jax.numpy as jnp
from jax import lax
from jax.sharding import Mesh
from jax.sharding import PartitionSpec as P

QUERY_HEADS = 32
KEY_VALUE_HEADS = 4
HEAD_WIDTH = 128
DP_EXPERT = ("dp", "expert_0", "expert_1")
DP_SEQ = ("dp", "seq_0", "seq_1")
SEQ = ("seq_0", "seq_1")
DP_SEQ_EXPERT = ("dp", "seq_0", "seq_1", "expert_0", "expert_1")
EXPERT = ("expert_0", "expert_1")
ROWS = DP_SEQ_EXPERT
MASKED = -1e30
EPSILON = 1e-06


def joined_along(blocks, dim):
    blocks = jnp.moveaxis(blocks, 0, dim)
    lengths = blocks.shape
    return blocks.reshape(*lengths[:dim], lengths[dim] * lengths[dim + 1], *lengths[dim + 2 :])


def from_everyone(array, axis):
    copies = jnp.broadcast_to(array, (lax.axis_size(axis), *array.shape))
    return lax.all_to_all(copies, axis, split_axis=0, concat_axis=0, tiled=True)


def gather_directly(array, axis, dim):
    return joined_along(from_everyone(array, axis), dim)


def in_blocks(array, dim, count):
    lengths = array.shape
    blocks = array.reshape(*lengths[:dim], count, lengths[dim] // count, *lengths[dim + 1 :])
    return jnp.moveaxis(blocks, dim, 0)


def sent_and_summed(array, axis, dim):
    count = lax.axis_size(axis)
    blocks = lax.all_to_all(in_blocks(array, dim, count), axis, 0, 0, tiled=True)
    return jnp.sum(blocks.astype(jnp.float32), axis=0)


def rms_scale(stream):
    return lax.rsqrt(jnp.mean(stream * stream, axis=-1, keepdims=True) + EPSILON)


def head_logit(final, head_vec):
    return jnp.sum(final * rms_scale(final) * head_vec.astype(jnp.float32)[None, :], axis=1)


def split_pair(value):
    high = value.astype(jnp.bfloat16)
    low = (value - high.astype(jnp.float32)).astype(jnp.bfloat16)
    return (high, low)


def join_pair(high, low):
    return high.astype(jnp.float32) + low.astype(jnp.float32)


def merge_heads(weighted_r, totals_r, peak_r):
    peak_all = jnp.max(peak_r, axis=0)
    factor = jnp.exp(peak_r - peak_all[None])
    weighted_sum = jnp.sum(weighted_r * factor[..., None], axis=0)
    totals_sum = jnp.sum(totals_r * factor, axis=0)
    merged = weighted_sum / totals_sum[..., None]
    return merged.reshape(merged.shape[0], -1).astype(jnp.bfloat16)


def shards(
    keys,
    values,
    queries,
    residual,
    out_proj,
    norm_gain,
    router,
    w_gate,
    w_up,
    w_down,
    head_vec,
    routes,
    step_pos,
    labels,
    trace_len,
):
    block_routes = lax.all_gather(routes[0], DP_EXPERT, axis=0)
    block_routes = block_routes.reshape(
        lax.axis_size("dp"), lax.axis_size(EXPERT), *routes.shape[1:]
    )
    routes_all = jnp.swapaxes(block_routes, 1, 2).reshape(-1, routes.shape[2])
    count_of_keys = keys.shape[1]
    query_groups = QUERY_HEADS // KEY_VALUE_HEADS
    query_all = gather_directly(queries, DP_SEQ, 1)[0]
    positions = step_pos[0]
    number_of_steps = positions.shape[0]
    lengths = trace_len[0]
    trace_ends = jnp.cumsum(lengths)
    starts = jnp.sum(
        jnp.where(trace_ends[None, :] <= positions[:, None], lengths[None, :], 0), axis=1
    )
    key_pos = lax.axis_index(DP_SEQ) * count_of_keys + jnp.arange(count_of_keys, dtype=jnp.int32)
    allowed = (key_pos[None, :] <= positions[:, None]) & (key_pos[None, :] >= starts[:, None])
    score_list = []
    for head_cluster in range(KEY_VALUE_HEADS):
        query_part = query_all[
            :,
            head_cluster
            * query_groups
            * HEAD_WIDTH : (head_cluster + 1)
            * query_groups
            * HEAD_WIDTH,
        ].reshape(number_of_steps * query_groups, HEAD_WIDTH)
        key_part = keys[0, :, head_cluster * HEAD_WIDTH : (head_cluster + 1) * HEAD_WIDTH]
        score_part = lax.dot_general(
            query_part, key_part, (((1,), (1,)), ((), ())), preferred_element_type=jnp.float32
        ) * HEAD_WIDTH ** (-0.5)
        score_part = score_part.reshape(number_of_steps, query_groups, count_of_keys)
        score_list.append(jnp.where(allowed[:, None, :], score_part, MASKED))
    scores = jnp.stack(score_list, axis=1).reshape(number_of_steps, QUERY_HEADS, count_of_keys)
    local_peak = jnp.max(scores, axis=2)
    heads_of_values = values[0].reshape(count_of_keys, KEY_VALUE_HEADS, HEAD_WIDTH)
    complete_weight_rows = jnp.where(
        allowed[:, None, :], jnp.exp(scores - local_peak[:, :, None]), 0.0
    )
    totals = jnp.sum(complete_weight_rows, axis=2)
    reduced_weight_rows = complete_weight_rows.astype(jnp.bfloat16).reshape(
        number_of_steps, KEY_VALUE_HEADS, query_groups, count_of_keys
    )
    weighted = jnp.einsum(
        "skgt,tkd->skgd", reduced_weight_rows, heads_of_values, preferred_element_type=jnp.float32
    ).reshape(number_of_steps, QUERY_HEADS, HEAD_WIDTH)
    totals_hi, totals_lo = split_pair(totals)
    peak_hi, peak_lo = split_pair(local_peak)
    packed = jnp.concatenate(
        [
            weighted.astype(jnp.bfloat16),
            totals_hi[..., None],
            totals_lo[..., None],
            peak_hi[..., None],
            peak_lo[..., None],
        ],
        axis=-1,
    )
    arrived = lax.all_to_all(
        packed.reshape(1, *packed.shape), DP_SEQ, split_axis=2, concat_axis=0, tiled=True
    )
    attn = merge_heads(
        arrived[..., :HEAD_WIDTH].astype(jnp.float32),
        join_pair(arrived[..., HEAD_WIDTH], arrived[..., HEAD_WIDTH + 1]),
        join_pair(arrived[..., HEAD_WIDTH + 2], arrived[..., HEAD_WIDTH + 3]),
    )
    mixed = sent_and_summed(
        jnp.dot(attn, out_proj, preferred_element_type=jnp.float32).astype(jnp.bfloat16), DP_SEQ, 0
    )
    stream = residual[0].astype(jnp.float32) + mixed
    normed = (stream * rms_scale(stream) * norm_gain.astype(jnp.float32)[None, :]).astype(
        jnp.bfloat16
    )
    normed_all = lax.all_gather(normed, ROWS, axis=0, tiled=True)
    experts = router.shape[1]
    logits = jnp.dot(normed_all, router, preferred_element_type=jnp.float32)
    chosen = (routes_all[:, :, None] == jnp.arange(experts, dtype=jnp.int32)[None, None, :]).astype(
        jnp.float32
    )
    picked = jnp.sum(chosen * logits[:, None, :], axis=2)
    gate_weight = jax.nn.softmax(picked, axis=-1)
    mine = routes_all == lax.axis_index(DP_EXPERT)
    coef = jnp.sum(jnp.where(mine, gate_weight, 0.0), axis=1)
    gate_act = jnp.dot(normed_all, w_gate[0], preferred_element_type=jnp.float32)
    up_act = jnp.dot(normed_all, w_up[0], preferred_element_type=jnp.float32)
    hidden = (jax.nn.silu(gate_act) * up_act).astype(jnp.bfloat16)
    expert_out = jnp.dot(hidden, w_down[0], preferred_element_type=jnp.float32)
    expert_mix = lax.psum_scatter(coef[:, None] * expert_out, ROWS, scatter_dimension=0, tiled=True)
    final = stream + expert_mix
    reward, pull = jax.vjp(lambda value: head_logit(value, head_vec), final)
    target = labels[0].astype(jnp.float32)
    loss_term = jax.nn.softplus(reward) - target * reward
    logit_grad = jax.nn.sigmoid(reward) - target
    (final_grad,) = pull(logit_grad)
    d_mix = final_grad.astype(jnp.bfloat16)
    d_mix_all = lax.all_gather(d_mix, ROWS, axis=0, tiled=True)
    d_mix_wide = d_mix_all.astype(jnp.float32)
    contract_rows = (((0,), (0,)), ((), ()))
    d_out = (coef[:, None] * d_mix_wide).astype(jnp.bfloat16)
    grad_down = lax.dot_general(hidden, d_out, contract_rows, preferred_element_type=jnp.float32)
    grad_down = grad_down.astype(jnp.bfloat16).reshape((1,) + grad_down.shape)
    share_dot = jnp.sum(d_mix_wide * expert_out, axis=1)
    row_count = normed_all.shape[0]
    own_row = jnp.arange(row_count, dtype=jnp.int32) == lax.axis_index(ROWS)
    payload = jnp.concatenate(
        [jnp.where(mine, share_dot[:, None], 0.0), jnp.where(own_row, loss_term, 0.0)[:, None]],
        axis=1,
    )
    summed = lax.psum(payload, ROWS)
    route_dot = summed[:, :-1]
    loss = jnp.sum(summed[:, -1])
    pick_grad = gate_weight * (route_dot - jnp.sum(gate_weight * route_dot, axis=1, keepdims=True))
    d_logits = jnp.sum(chosen * pick_grad[:, :, None], axis=1)
    router_grad_all = lax.dot_general(
        normed_all.astype(jnp.float32), d_logits, contract_rows, precision=lax.Precision.HIGHEST
    )
    own_rows = router_grad_all.shape[0] // lax.axis_size(DP_SEQ_EXPERT)
    grad_router = lax.dynamic_slice_in_dim(
        router_grad_all, lax.axis_index(DP_SEQ_EXPERT) * own_rows, own_rows, axis=0
    ).astype(jnp.bfloat16)
    return (loss, grad_down, grad_router)


def solution(mesh):
    finer = Mesh(
        mesh.devices.reshape(mesh.shape["dp"], 2, 2, 4, 4),
        ("dp", "seq_0", "seq_1", "expert_0", "expert_1"),
    )
    return jax.shard_map(
        shards,
        mesh=finer,
        in_specs=(
            P(EXPERT, DP_SEQ, None),
            P(EXPERT, DP_SEQ, None),
            P(EXPERT, DP_SEQ, None),
            P(EXPERT, DP_SEQ, None),
            P(DP_SEQ, None),
            P(),
            P(),
            P(DP_EXPERT, None, SEQ),
            P(DP_EXPERT, None, SEQ),
            P(DP_EXPERT, SEQ, None),
            P(),
            P(EXPERT, "dp", None),
            P(EXPERT, None),
            P(EXPERT, DP_SEQ),
            P(EXPERT, None),
        ),
        out_specs=(P(), P(DP_EXPERT, SEQ, None), P(DP_SEQ_EXPERT, None)),
        check_vma=False,
    )
```

profile of v0, /device:TPU:1, one launch (start us, length us, event | category | flops | bytes accessed | tf_op | source)
XLA Modules:
  0.0 3206.8 jit_solution(4722802899857417348)
XLA Ops:
  7.2 0.8 reduce.14
  8.1 0.5 broadcast_in_dim.130
  8.5 0.5 broadcast.181
  9.0 2.2 reduce.15
  11.3 0.9 reshape.490
  12.1 16.7 all-to-all-start
  29.3 18.7 all-to-all-done
  52.1 0.6 concatenate.6
  53.0 32.4 %all_to_all.28 = bf16[1,32,32,132]{3,1,0,2:T(8,128)(2,1)S(1)} all-to-all(bf16[1,32,32,132]{3,1,0,2:T(8,128)(2,1)S(1)} %copy.165), channel_id=1, replica_groups=mesh['dp'=8,'seq_0'=2,'seq_1'=2,'expert_0'=4,'expert_1'=4] {'dp','seq_0'..., dimensions={2} | all-to-all | bytes 540672 | tf_op jit(solution)/shard_map/all_to_all | solution.py:149
  85.4 1.1 copy.166
  86.6 0.5 multiply_reduce_fusion
  87.3 0.7 reduce.16
  88.0 0.7 reshape.492
  88.7 9.7 all-to-all-start.2
  98.5 15.2 all-to-all-done.2
  114.0 0.6 copy-done.9
  114.6 0.6 multiply_reduce_fusion.5
  115.9 0.6 multiply_convert_fusion
  116.6 462.9 %all_gather.9 = s32[128,4,8]{2,1,0:T(4,128)S(1)} all-gather(s32[1,4,8]{2,1,0:T(4,128)S(1)} %copy-done.17), channel_id=1, replica_groups=mesh['dp'=8,'seq_0'=2,'seq_1'=2,'expert_0'=4,'expert_1'=4] {'dp','expert..., dimensions={0}, use_global_device_ids=true | all-gather | bytes 16512 | tf_op jit(solution)/shard_map/all_gather | solution.py:91
  580.5 593.1 %all-gather.5.cloned.1.call-done = bf16[1048576]{0:T(1024)(128)(2,1)} async-done(((bf16[2048]{0:T(1024)(128)(2,1)}), bf16[1048576]{0:T(1024)(128)(2,1)}) %all-gather.5.cloned.1.call-update) | async-done | bytes 2097168 | tf_op jit(solution)/shard_map/all_gather | solution.py:164
  1173.6 2.8 reshape.484
  1176.4 2.8 fusion.21
  1179.2 0.7 fusion.51
  1179.9 7.3 select_reduce_fusion.1
  1187.3 0.8 reduce_max.32
  1188.1 1.4 sub.91
  1189.4 1.3 fusion.45
  1190.7 1.4 div.48
  1192.1 1.3 copy.173
  1193.4 0.8 copy.171
  1194.2 0.7 copy.170
  1194.9 0.9 select_reduce_fusion.2
  1195.9 2.1 fusion.7
  1198.0 4.1 broadcast_multiply_fusion
  1202.2 0.6 copy-done.15
  1203.5 480.3 %all-reduce.3.cloned.1.call-done = f32[512,2048]{1,0:T(8,128)} async-done(((f32[512,2048]{1,0:T(8,128)}), f32[512,2048]{1,0:T(8,128)}) %all-reduce.3.cloned.1.call-update) | async-done | bytes 4194320
  1683.8 1.5 multiply_reduce_fusion.4
  1686.0 0.6 multiply_reduce_fusion.3
  1687.3 0.6 multiply_reduce_fusion.2
  1688.6 0.6 fusion.47
  1693.2 1384.5 %all-gather.7.cloned.1.call-done = bf16[512,1,2048]{2,1,0:T(2,128)(2,1)} async-done(((bf16[1,1,2048]{2,1,0:T(2,128)(2,1)}), bf16[512,1,2048]{2,1,0:T(2,128)(2,1)}) %all-gather.7.cloned.1.call-update) | async-done | bytes 2097168 | tf_op jit(solution)/shard_map/all_gather | solution.py:186
  3077.8 4.8 fusion
  3082.6 106.9 %psum.7 = f32[512,9]{0,1:T(8,128)S(1)} all-reduce(f32[512,9]{0,1:T(8,128)S(1)} %pad_maximum_fusion.2), channel_id=1, replica_groups=mesh['dp'=8,'seq_0'=2,'seq_1'=2,'expert_0'=4,'expert_1'=4] {'dp','seq_0'..., use_global_device_ids=true, to_apply=%region_18.19 | all-reduce | flops 4608 | bytes 36864 | tf_op jit(solution)/shard_map/psum | solution.py:199
  3189.6 0.6 slice_reduce_fusion
  3190.3 2.5 select_reduce_fusion
  3192.8 2.3 fusion.52
  3195.1 0.6 dynamic-slice_convert_fusion
  3195.7 4.6 fusion.2
  (97 shorter events, 6.9 us)
Async XLA Ops:
  7.2 1190.9 %copy-start = (bf16[1,192,2048]{2,1,0:T(8,128)(2,1)S(1)}, bf16[1,192,2048]{2,1,0:T(8,128)(2,1)}, u32[]{:S(2)}) copy-start(bf16[1,192,2048]{2,1,0:T(8,128)(2,1)} %param.24) | copy-start | bytes 2359300
  7.2 21.7 copy-start.8
  7.2 21.8 copy-start.19
  7.2 22.0 copy-start.18
  9.0 39.7 %copy-start.7 = (bf16[1,128,512]{2,1,0:T(8,128)(2,1)S(1)}, bf16[1,128,512]{2,1,0:T(8,128)(2,1)}, u32[]{:S(2)}) copy-start(bf16[1,128,512]{2,1,0:T(8,128)(2,1)} %param.15) | copy-start | bytes 393220
  12.1 35.9 %all-to-all-start = ((bf16[32,2,2048]{2,1,0:T(2,128)(2,1)}), bf16[32,2,2048]{2,1,0:T(2,128)(2,1)S(1)}, u32[]{:S(2)}, u32[]{:S(2)}) async-start(bf16[32,2,2048]{2,1,0:T(2,128)(2,1)} %reshape.490), calls=%async_computation | async-start | bytes 524288 | tf_op jit(solution)/shard_map/all_to_all | solution.py:28
  53.0 34.1 %copy-start.1 = (bf16[128,2048]{1,0:T(8,128)(2,1)S(1)}, bf16[128,2048]{1,0:T(8,128)(2,1)}, u32[]{:S(2)}) copy-start(bf16[128,2048]{1,0:T(8,128)(2,1)} %param.19) | copy-start | bytes 1572868
  85.3 13.1 copy-start.13
  86.5 29.4 copy-start.16
  86.5 30.1 copy-start.17
  88.7 25.0 all-to-all-start.2
  98.4 1075.2 %all-gather.5.cloned.1.call-start = ((), (), s32[]{:S(2)}) async-start(), calls=%async_computation.3 | async-start | bytes 2101248 | tf_op jit(solution)/shard_map/all_gather | solution.py:164
  114.0 0.6 copy-start.9
  116.5 1567.2 %all-reduce.3.cloned.1.call-start = ((), (), s32[]{:S(2)}) async-start(), calls=%async_computation.5 | async-start | bytes 8388608
  579.9 0.6 copy-start.5
  1176.4 2.8 copy-start.2
  1198.0 4.1 copy-start.3
  1202.1 0.7 copy-start.15
  1202.1 481.7 %copy-start.10 = (f32[2048]{0:T(1024)S(1)}, f32[2048]{0:T(1024)}, u32[]{:S(2)}) copy-start(f32[2048]{0:T(1024)} %copy-done.9) | copy-start | bytes 24580
  1202.1 481.7 %copy-start.14 = (bf16[1,1,2048]{2,1,0:T(2,128)(2,1)S(1)}, bf16[1,1,2048]{2,1,0:T(2,128)(2,1)}, u32[]{:S(2)}) copy-start(bf16[1,1,2048]{2,1,0:T(2,128)(2,1)} %param.18) | copy-start | bytes 12292
  1202.2 1875.6 %all-gather.7.cloned.1.call-start = ((), (), s32[]{:S(2)}) async-start(), calls=%async_computation.4 | async-start | bytes 4202496 | tf_op jit(solution)/shard_map/all_gather | solution.py:186
  3077.8 4.8 copy-start.6
  3077.8 111.8 %copy-start.11 = (f32[512]{0:T(512)S(1)}, f32[512]{0:T(512)}, u32[]{:S(2)}) copy-start(f32[512]{0:T(512)} %reduce_max.32) | copy-start | bytes 6148
  3077.8 111.8 %copy-start.12 = (f32[512]{0:T(512)S(1)}, f32[512]{0:T(512)}, u32[]{:S(2)}) copy-start(f32[512]{0:T(512)} %fusion.45) | copy-start | bytes 6148
  3190.3 5.4 copy-start.4
Sparse Core Ops, SparseCore 0:
  116.7 1056.8 all-gather.4
  1202.3 481.4 all-reduce.2
  1689.4 1388.3 all-gather.6
where the time goes:
time: 3210 us
  waiting for transfers between devices  2490 us (78%)
  blocking collectives  602 us (19%)
    all_gather x1, waiting for transfers between devices, shards(): d_mix_all = lax.all_gather(d_mix, ROWS, axis=0, tiled=True)  1380 us
    all_gather x1, waiting for transfers between devices, shards(): normed_all = lax.all_gather(normed, ROWS, axis=0, tiled=True)  593 us
    unnamed x4, waiting for transfers between devices  480 us
    all_gather x1, blocking collectives, shards(): block_routes = lax.all_gather(routes[0], DP_EXPERT, axis=0)  463 us
    psum x1, blocking collectives, shards(): summed = lax.psum(payload, ROWS)  107 us
  transfers between devices with their start and end apart: 5, of which 5 were waited for; matrix products, arithmetic and copies ran while one was open for 0% of the time, Pallas kernels for 0%

commit v1 on v0

--- a/solution.py
+++ b/solution.py
@@ -183,7 +183,8 @@
     logit_grad = jax.nn.sigmoid(reward) - target
     (final_grad,) = pull(logit_grad)
     d_mix = final_grad.astype(jnp.bfloat16)
-    d_mix_all = lax.all_gather(d_mix, ROWS, axis=0, tiled=True)
+    sent = jnp.stack([d_mix] * lax.axis_size(ROWS))
+    d_mix_all = jnp.concatenate(lax.all_to_all(sent, ROWS, 0, 0), axis=0)
     d_mix_wide = d_mix_all.astype(jnp.float32)
     contract_rows = (((0,), (0,)), ((), ()))
     d_out = (coef[:, None] * d_mix_wide).astype(jnp.bfloat16)

time: 3210 us -> 1970 us (0.61)
  waiting for transfers between devices: 2490 us -> 1200 us
    all_gather x1 -> x0, waiting for transfers between devices: 1380 us -> none  [shards(): d_mix_all = lax.all_gather(d_mix, ROWS, axis=0, tiled=True)]
    all_to_all x0 -> x1, waiting for transfers between devices: none -> 95.6 us  [shards(): d_mix_all = jnp.concatenate(lax.all_to_all(sent, ROWS, 0, 0), axis=0)]
    unnamed x4 -> x3, waiting for transfers between devices: 480 us -> 480 us
where the time goes in v1:
time: 1970 us
  waiting for transfers between devices  1200 us (61%)
  blocking collectives  595 us (30%)
  starting transfers between devices  47.6 us (2%)
  other arithmetic  41.1 us (2%)
  local copies, waits for them, and re-layouts  40.7 us (2%)
  between operations  22 us (1%)
    all_gather x1, waiting for transfers between devices, shards(): normed_all = lax.all_gather(normed, ROWS, axis=0, tiled=True)  593 us
    unnamed x3, waiting for transfers between devices  480 us
    all_gather x1, blocking collectives, shards(): block_routes = lax.all_gather(routes[0], DP_EXPERT, axis=0)  463 us
    psum x1, blocking collectives, shards(): summed = lax.psum(payload, ROWS)  100 us
    all_to_all x1, waiting for transfers between devices, shards(): d_mix_all = jnp.concatenate(lax.all_to_all(sent, ROWS, 0, 0), axis=0)  95.6 us
  transfers between devices with their start and end apart: 5, of which 5 were waited for; matrix products, arithmetic and copies ran while one was open for 0% of the time, Pallas kernels for 0%

profile of v1, /device:TPU:1, one launch (start us, length us, event | category | flops | bytes accessed | tf_op | source)
XLA Modules:
  0.0 1967.6 jit_solution(6742099308731557947)
XLA Ops:
  7.2 0.8 reduce.14
  9.0 2.2 reduce.17
  11.3 0.9 reshape.495
  12.1 16.7 all-to-all-start
  29.3 18.7 all-to-all-done
  52.9 32.4 %all_to_all.33 = bf16[1,32,32,132]{3,1,0,2:T(8,128)(2,1)S(1)} all-to-all(bf16[1,32,32,132]{3,1,0,2:T(8,128)(2,1)S(1)} %copy.165), channel_id=1, replica_groups=mesh['dp'=8,'seq_0'=2,'seq_1'=2,'expert_0'=4,'expert_1'=4] {'dp','seq_0'..., dimensions={2} | all-to-all | bytes 540672 | tf_op jit(solution)/shard_map/all_to_all | solution.py:149
  85.3 1.1 copy.166
  87.3 0.7 reduce.18
  88.0 0.7 reshape.497
  88.7 9.7 all-to-all-start.2
  98.5 15.2 all-to-all-done.2
  114.0 0.6 copy-done.8
  114.6 0.6 multiply_reduce_fusion.5
  115.9 0.6 multiply_convert_fusion
  116.6 462.9 %all_gather.6 = s32[128,4,8]{2,1,0:T(4,128)S(1)} all-gather(s32[1,4,8]{2,1,0:T(4,128)S(1)} %copy-done.16), channel_id=1, replica_groups=mesh['dp'=8,'seq_0'=2,'seq_1'=2,'expert_0'=4,'expert_1'=4] {'dp','expert..., dimensions={0}, use_global_device_ids=true | all-gather | bytes 16512 | tf_op jit(solution)/shard_map/all_gather | solution.py:91
  580.4 593.1 %all-gather.3.cloned.1.call-done = bf16[1048576]{0:T(1024)(128)(2,1)} async-done(((bf16[2048]{0:T(1024)(128)(2,1)}), bf16[1048576]{0:T(1024)(128)(2,1)}) %all-gather.3.cloned.1.call-update) | async-done | bytes 2097168 | tf_op jit(solution)/shard_map/all_gather | solution.py:164
  1173.5 2.8 reshape.491
  1176.4 2.8 fusion.21
  1179.1 0.7 fusion.51
  1179.9 7.3 select_reduce_fusion.1
  1187.3 0.8 reduce_max.32
  1188.0 1.4 sub.91
  1189.4 1.3 fusion.45
  1190.7 1.4 div.48
  1192.0 1.3 copy.173
  1193.3 0.8 copy.171
  1194.1 0.7 copy.170
  1194.8 0.9 select_reduce_fusion.2
  1195.9 2.1 fusion.7
  1198.0 4.1 broadcast_multiply_fusion
  1202.1 0.6 copy-done.14
  1203.4 480.3 %all-reduce.3.cloned.1.call-done = f32[512,2048]{1,0:T(8,128)} async-done(((f32[512,2048]{1,0:T(8,128)}), f32[512,2048]{1,0:T(8,128)}) %all-reduce.3.cloned.1.call-update) | async-done | bytes 4194320
  1683.7 1.5 multiply_reduce_fusion.4
  1685.9 0.6 multiply_reduce_fusion.3
  1687.3 0.6 multiply_reduce_fusion.2
  1688.6 4.1 stack.5
  1692.7 14.5 reduce.19
  1707.3 4.5 reshape.499
  1711.8 21.1 %all-to-all-start.3 = ((bf16[512,2,1024]{2,1,0:T(2,128)(2,1)}), bf16[512,2,1024]{2,1,0:T(2,128)(2,1)}, u32[]{:S(2)}, u32[]{:S(2)}) async-start(bf16[512,2,1024]{2,1,0:T(2,128)(2,1)} %reshape.499), calls=%async_computation.3 | async-start | bytes 4194304 | tf_op jit(solution)/shard_map/all_to_all | solution.py:187
  1736.9 95.6 %all-to-all-done.3 = bf16[512,2,1024]{2,1,0:T(2,128)(2,1)} async-done(((bf16[512,2,1024]{2,1,0:T(2,128)(2,1)}), bf16[512,2,1024]{2,1,0:T(2,128)(2,1)}, u32[]{:S(2)}, u32[]{:S(2)}) %all-to-all-start.3) | async-done | bytes 2097184 | tf_op jit(solution)/shard_map/all_to_all | solution.py:187
  1832.5 13.6 reshape.500
  1846.1 4.7 fusion.2
  1850.8 3.7 fusion
  1854.6 100.0 %psum.7 = f32[512,9]{0,1:T(8,128)S(1)} all-reduce(f32[512,9]{0,1:T(8,128)S(1)} %pad_maximum_fusion.2), channel_id=1, replica_groups=mesh['dp'=8,'seq_0'=2,'seq_1'=2,'expert_0'=4,'expert_1'=4] {'dp','seq_0'..., use_global_device_ids=true, to_apply=%region_18.19 | all-reduce | flops 4608 | bytes 36864 | tf_op jit(solution)/shard_map/psum | solution.py:200
  1954.6 0.6 slice_reduce_fusion
  1955.3 2.5 select_reduce_fusion
  1957.8 2.3 fusion.52
  1960.1 0.6 dynamic-slice_convert_fusion
  (98 shorter events, 8.8 us)
Async XLA Ops:
  7.2 1190.8 %copy-start = (bf16[1,192,2048]{2,1,0:T(8,128)(2,1)S(1)}, bf16[1,192,2048]{2,1,0:T(8,128)(2,1)}, u32[]{:S(2)}) copy-start(bf16[1,192,2048]{2,1,0:T(8,128)(2,1)} %param.24) | copy-start | bytes 2359300
  7.2 21.7 %copy-start.7 = (bf16[1,128,512]{2,1,0:T(8,128)(2,1)S(1)}, bf16[1,128,512]{2,1,0:T(8,128)(2,1)}, u32[]{:S(2)}) copy-start(bf16[1,128,512]{2,1,0:T(8,128)(2,1)} %param.16) | copy-start | bytes 393220
  7.2 21.8 %copy-start.18 = (s32[1,8]{1,0:T(1,128)S(1)}, s32[1,8]{1,0:T(1,128)}, u32[]{:S(2)}) copy-start(s32[1,8]{1,0:T(1,128)} %param.29) | copy-start | bytes 100
  7.2 22.0 %copy-start.17 = (s32[1,32]{1,0:T(1,128)S(1)}, s32[1,32]{1,0:T(1,128)}, u32[]{:S(2)}) copy-start(s32[1,32]{1,0:T(1,128)} %param.27) | copy-start | bytes 388
  9.0 39.7 %copy-start.6 = (bf16[1,128,512]{2,1,0:T(8,128)(2,1)S(1)}, bf16[1,128,512]{2,1,0:T(8,128)(2,1)}, u32[]{:S(2)}) copy-start(bf16[1,128,512]{2,1,0:T(8,128)(2,1)} %param.15) | copy-start | bytes 393220
  12.1 35.9 %all-to-all-start = ((bf16[32,2,2048]{2,1,0:T(2,128)(2,1)}), bf16[32,2,2048]{2,1,0:T(2,128)(2,1)S(1)}, u32[]{:S(2)}, u32[]{:S(2)}) async-start(bf16[32,2,2048]{2,1,0:T(2,128)(2,1)} %reshape.495), calls=%async_computation | async-start | bytes 524288 | tf_op jit(solution)/shard_map/all_to_all | solution.py:28
  52.9 34.1 %copy-start.2 = (bf16[128,2048]{1,0:T(8,128)(2,1)S(1)}, bf16[128,2048]{1,0:T(8,128)(2,1)}, u32[]{:S(2)}) copy-start(bf16[128,2048]{1,0:T(8,128)(2,1)} %param.19) | copy-start | bytes 1572868
  85.3 13.1 copy-start.12
  86.4 29.4 %copy-start.15 = (bf16[2048]{0:T(1024)(128)(2,1)S(1)}, bf16[2048]{0:T(1024)(128)(2,1)}, u32[]{:S(2)}) copy-start(bf16[2048]{0:T(1024)(128)(2,1)} %param.20) | copy-start | bytes 12292
  86.5 30.1 %copy-start.16 = (s32[1,4,8]{2,1,0:T(4,128)S(1)}, s32[1,4,8]{2,1,0:T(4,128)}, u32[]{:S(2)}) copy-start(s32[1,4,8]{2,1,0:T(4,128)} %param.26) | copy-start | bytes 388
  88.7 25.0 %all-to-all-start.2 = ((bf16[32,2,1024]{2,1,0:T(2,128)(2,1)}), bf16[32,2,1024]{2,1,0:T(2,128)(2,1)S(1)}, u32[]{:S(2)}, u32[]{:S(2)}) async-start(bf16[32,2,1024]{2,1,0:T(2,128)(2,1)} %reshape.497), calls=%async_computation.2 | async-start | bytes 262144 | tf_op jit(solution)/shard_map/all_to_all | solution.py:43
  98.4 1075.1 %all-gather.3.cloned.1.call-start = ((), (), s32[]{:S(2)}) async-start(), calls=%async_computation.4 | async-start | bytes 2101248 | tf_op jit(solution)/shard_map/all_gather | solution.py:164
  114.0 0.6 copy-start.8
  116.5 1567.2 %all-reduce.3.cloned.1.call-start = ((), (), s32[]{:S(2)}) async-start(), calls=%async_computation.5 | async-start | bytes 8388608
  579.8 0.6 copy-start.4
  1176.3 2.8 copy-start.3
  1202.1 0.7 copy-start.14
  1202.1 481.7 %copy-start.9 = (f32[2048]{0:T(1024)S(1)}, f32[2048]{0:T(1024)}, u32[]{:S(2)}) copy-start(f32[2048]{0:T(1024)} %copy-done.8) | copy-start | bytes 24580
  1202.1 481.7 %copy-start.13 = (bf16[1,1,2048]{2,1,0:T(2,128)(2,1)S(1)}, bf16[1,1,2048]{2,1,0:T(2,128)(2,1)}, u32[]{:S(2)}) copy-start(bf16[1,1,2048]{2,1,0:T(2,128)(2,1)} %param.18) | copy-start | bytes 12292
  1711.8 120.7 %all-to-all-start.3 = ((bf16[512,2,1024]{2,1,0:T(2,128)(2,1)}), bf16[512,2,1024]{2,1,0:T(2,128)(2,1)}, u32[]{:S(2)}, u32[]{:S(2)}) async-start(bf16[512,2,1024]{2,1,0:T(2,128)(2,1)} %reshape.499), calls=%async_computation.3 | async-start | bytes 4194304 | tf_op jit(solution)/shard_map/all_to_all | solution.py:187
  1846.1 4.7 copy-start.1
  1850.8 3.7 copy-start.5
  1850.8 103.7 %copy-start.10 = (f32[512]{0:T(512)S(1)}, f32[512]{0:T(512)}, u32[]{:S(2)}) copy-start(f32[512]{0:T(512)} %reduce_max.32) | copy-start | bytes 6148
  1850.8 103.7 %copy-start.11 = (f32[512]{0:T(512)S(1)}, f32[512]{0:T(512)}, u32[]{:S(2)}) copy-start(f32[512]{0:T(512)} %fusion.45) | copy-start | bytes 6148
Sparse Core Ops, SparseCore 0:
  116.6 1056.8 all-gather.2
  1202.2 481.4 all-reduce.2
